TPU v7x, 128 devices: a whole 4x4x4 slice. The times are simulated.
128 devices in a mesh: seq: 16 (over x_hi, z, core), kvh: 8 (over x_lo, y).
Axes of the slice: x: 4 (x_hi: 2, x_lo: 2; x = x_hi * 2 + x_lo), y: 4, z: 4, core: 2. Of those that a mesh axis runs over, the one named last changes fastest.
Arguments:
- normed: bfloat16 [4096, 4096], P('seq'), may hold values from -8 to 8
- w_query: bfloat16 [4096, 4096], P(None, 'kvh'), may hold values from -1 to 1, as said below
- w_key: bfloat16 [4096, 1024], P(None, 'kvh'), may hold values from -1 to 1, as said below
- w_value: bfloat16 [4096, 1024], P(None, 'kvh'), may hold values from -0.09375 to 0.09375
- positions: int32 [4096], P('seq'), may hold values from 0 to 4222, as said below
- block_mask: int32 [32, 32], P('seq'), may hold values from 0 to 1, as said below
- grad_attn: bfloat16 [4096, 4096], P('seq', 'kvh'), may hold values from -6 to 6
Outputs:
- grad_normed: bfloat16 [4096, 4096], P('seq', 'kvh')
- grad_wq: float32 [4096, 4096], P('seq', 'kvh')
- grad_wk: float32 [4096, 1024], P('seq', 'kvh')
- grad_wv: float32 [4096, 1024], P('seq', 'kvh')
Inputs may be any that keep to these rules, and one draw needn't show every extreme that they name: Within a block positions rise by one per token; block b starts between b * 128 and (b + 1) * 128 - 1, block 0 at 0, the last block at its latest start. `block_mask`: the diagonal is 1; a block may read only blocks of earlier rounds besides itself; entries for earlier rounds are 0 or 1. `w_query`: entries of about 4096^(-1/2) in size. `w_key`: entries of about 4096^(-1/2) in size.
All inputs are finite; a program needn't handle non-finite values.
Results may differ from a plain program's by a relative error of at most 0.019.
The roundings to bfloat16 on the way count: a program that leaves them out, or rounds other values in their place, can miss the bound.
Values may be sent and summed in bfloat16 or wider, within the bound.
No kernel may reach another device: no remote copies, remote signals or barrier semaphores. Data moves between devices by JAX's collectives and lax.ppermute only.
A program may use at most 128 MiB of HBM per device.

v0:
```python
import jax
import jax.numpy as jnp
from jax import lax
from jax.sharding import PartitionSpec as P

HEAD = 128
BLOCK = 128
THETA = 500000.0


def rotate(values, positions, rotation_sign):
    tok_rows = values.shape[0]
    head_count = values.shape[1] // HEAD
    half_size = HEAD // 2
    pieces = values.reshape(tok_rows, head_count, HEAD)
    frequency = THETA ** (-(jnp.arange(half_size, dtype=jnp.float32) * (2.0 / HEAD)))
    angles = positions.astype(jnp.float32)[:, None] * frequency[None, :]
    cosine = jnp.cos(angles)[:, None, :]
    sine_part = rotation_sign * jnp.sin(angles)[:, None, :]
    lower_half = pieces[:, :, :half_size]
    upper_half = pieces[:, :, half_size:]
    turned = jnp.concatenate(
        [
            lower_half * cosine - upper_half * sine_part,
            upper_half * cosine + lower_half * sine_part,
        ],
        axis=2,
    )
    return turned.reshape(tok_rows, head_count * HEAD)


def visible(mask_table, query_block0, query_count, key_count):
    query_local = jnp.arange(query_count)
    key_local = jnp.arange(key_count)
    query_block = query_block0 + query_local // BLOCK
    key_block = key_local // BLOCK
    allowed = jnp.repeat(jnp.repeat(mask_table, BLOCK, axis=0), BLOCK, axis=1) == 1
    inner_ok = (key_local % BLOCK)[None, :] <= (query_local % BLOCK)[:, None]
    return allowed & ((query_block[:, None] != key_block[None, :]) | inner_ok)


def product(form, left, right):
    return jnp.einsum(form, left, right, preferred_element_type=jnp.float32)


def masked_scores(queries, keys, seen):
    scores = product("tgd,sd->gts", queries, keys) * HEAD ** (-0.5)
    return jnp.where(seen[None], scores, -1e30)


def softmax_stats(queries, keys, values, grad_heads, seen):
    scores = masked_scores(queries, keys, seen)
    row_max = jnp.max(scores, axis=2, keepdims=True)
    log_total = row_max[:, :, 0] + jnp.log(jnp.sum(jnp.exp(scores - row_max), axis=2))
    weights = jnp.where(seen[None], jnp.exp(scores - log_total[:, :, None]), 0.0).astype(
        jnp.bfloat16
    )
    outputs = product("gts,sd->gtd", weights, values)
    row_dots = jnp.sum(outputs * jnp.transpose(grad_heads.astype(jnp.float32), (1, 0, 2)), axis=2)
    return (log_total, row_dots)


def attention_grads(queries, keys, values, grad_heads, seen, log_total, row_dots):
    scores = masked_scores(queries, keys, seen)
    probs = jnp.where(seen[None], jnp.exp(scores - log_total[:, :, None]), 0.0)
    weights = probs.astype(jnp.bfloat16)
    grad_probs = product("tgd,sd->gts", grad_heads, values)
    grad_scores = (probs * (grad_probs - row_dots[:, :, None]) * HEAD ** (-0.5)).astype(
        jnp.bfloat16
    )
    grad_query = product("gts,sd->tgd", grad_scores, keys)
    grad_key = product("gts,tgd->sd", grad_scores, queries)
    grad_value = product("gts,tgd->sd", weights, grad_heads)
    return (grad_query, grad_key, grad_value)


def body(normed, w_query, w_key, w_value, positions, block_mask, grad_attn):
    tok_rows = normed.shape[0]
    group_size = w_query.shape[1] // w_key.shape[1]
    width_query = group_size * HEAD
    blk_local = tok_rows // BLOCK
    my_index = lax.axis_index("seq")
    queries = rotate(
        jnp.dot(normed, w_query, preferred_element_type=jnp.float32), positions, 1.0
    ).astype(jnp.bfloat16)
    keys = rotate(
        jnp.dot(normed, w_key, preferred_element_type=jnp.float32), positions, 1.0
    ).astype(jnp.bfloat16)
    values = jnp.dot(normed, w_value, preferred_element_type=jnp.float32).astype(jnp.bfloat16)
    keys_all, values_all = (
        lax.all_gather(keys, "seq", axis=0, tiled=True),
        lax.all_gather(values, "seq", axis=0, tiled=True),
    )
    seen = visible(block_mask, my_index * blk_local, tok_rows, keys_all.shape[0])
    total_parts = []
    dots_parts = []
    query_heads = queries.reshape(tok_rows, group_size, HEAD)
    grad_heads = grad_attn.reshape(tok_rows, group_size, HEAD)
    log_total, row_dots = softmax_stats(query_heads, keys_all, values_all, grad_heads, seen)
    grad_query, grad_key, grad_value = attention_grads(
        query_heads, keys_all, values_all, grad_heads, seen, log_total, row_dots
    )
    query_parts = grad_query.reshape(tok_rows, width_query)
    total_parts.append(log_total.T)
    dots_parts.append(row_dots.T)
    key_total, value_total = (
        lax.psum_scatter(
            grad_key.astype(jnp.bfloat16), "seq", scatter_dimension=0, tiled=True
        ).astype(jnp.float32),
        lax.psum_scatter(
            grad_value.astype(jnp.bfloat16), "seq", scatter_dimension=0, tiled=True
        ).astype(jnp.float32),
    )
    query_grad = rotate(query_parts, positions, -1.0).astype(jnp.bfloat16)
    key_grad = rotate(key_total, positions, -1.0).astype(jnp.bfloat16)
    value_grad = value_total.astype(jnp.bfloat16)
    joined = jnp.concatenate([query_grad, key_grad, value_grad], axis=1)
    weight_grads = lax.psum_scatter(
        lax.dot_general(
            normed, joined, (((0,), (0,)), ((), ())), preferred_element_type=jnp.float32
        ).astype(jnp.bfloat16),
        "seq",
        scatter_dimension=0,
        tiled=True,
    ).astype(jnp.float32)
    query_cols = query_grad.shape[1]
    key_cols = key_grad.shape[1]
    grad_wq = weight_grads[:, :query_cols]
    grad_wk = weight_grads[:, query_cols : query_cols + key_cols]
    grad_wv = weight_grads[:, query_cols + key_cols :]
    contract = (((1,), (1,)), ((), ()))
    partial_input = lax.dot_general(
        query_grad, w_query, contract, preferred_element_type=jnp.float32
    )
    partial_input = partial_input + lax.dot_general(
        key_grad, w_key, contract, preferred_element_type=jnp.float32
    )
    partial_input = partial_input + lax.dot_general(
        value_grad, w_value, contract, preferred_element_type=jnp.float32
    )
    grad_normed = lax.psum_scatter(
        partial_input.astype(jnp.bfloat16), "kvh", scatter_dimension=1, tiled=True
    )
    return (grad_normed, grad_wq, grad_wk, grad_wv)


def solution(mesh):
    in_specs = (
        P("seq", None),
        P(None, "kvh"),
        P(None, "kvh"),
        P(None, "kvh"),
        P("seq"),
        P("seq", None),
        P("seq", "kvh"),
    )
    out_specs = (P("seq", "kvh"), P("seq", "kvh"), P("seq", "kvh"), P("seq", "kvh"))
    return jax.shard_map(body, mesh=mesh, in_specs=in_specs, out_specs=out_specs, check_vma=False)
```

profile of v0, /device:TPU:0, one launch (start us, length us, event | category | flops | bytes accessed | tf_op | source)
XLA Modules:
  0.0 413.1 jit_solution(13094747481903445248)
XLA Ops:
  7.2 0.0 copy-start
  7.2 0.0 all-gather.6.cloned.1.call-start
  7.2 0.8 convert_element_type.52
  8.1 0.7 copy-done
  8.8 2.1 convolution_bitcast_fusion.3
  10.9 0.3 fusion.34
  11.2 0.6 pad_maximum_fusion.2
  11.8 0.0 all-gather.6.cloned.1.call-update
  11.9 0.0 all-gather.4.cloned.1.call-start
  11.9 2.5 convolution_convert_fusion.1
  14.5 0.0 all-gather.4.cloned.1.call-update
  14.5 0.0 reduce-scatter.5.cloned.1.call-start
  14.5 1.2 broadcast_multiply_fusion
  15.8 0.6 fusion.37
  16.4 3.4 fusion.55
  19.8 0.2 reshape.293
  20.0 1.1 fusion.53
  21.1 0.6 and_select_fusion
  21.7 0.7 broadcast_compare_fusion
  22.4 0.1 copy.27
  22.5 0.1 broadcast_in_dim.30
  22.6 0.6 copy.63
  23.2 0.8 copy.31
  24.1 1.9 subtract_convert_fusion.1
  26.0 2.5 bitcast_and_fusion
  28.5 28.9 %all-gather.6.cloned.1.call-done = bf16[4096,1,128]{0,2,1:T(8,128)(2,1)} async-done(((bf16[256,1,128]{0,2,1:T(8,128)(2,1)}), bf16[4096,1,128]{0,2,1:T(8,128)(2,1)}) %all-gather.6.cloned.1.call-update) | async-done | bytes 1048592 | tf_op jit(solution)/shard_map/all_gather | solution.py:91
  57.4 4.5 %fusion.4 = (f32[4,256]{1,0:T(4,128)S(1)}, f32[4096,256,4]{1,0,2:T(8,128)S(1)}) fusion(pred[256,4096]{0,1:T(8,128)(4,1)S(1)} %bitcast_and_fusion, bf16[256,4,64]{2,0,1:T(8,128)(2,1)} %get-tuple-element.13, bf16[256,4,64]{2,0,1:T(8,128)(2,1)S(1)} %get-tuple-element.12, bf16[4096,1,128]{0,2,1:T(8,128)(2,1)} %all-gather.6.cloned.1.call-done), kind=kOutput, calls=%fused_computation.8 | convolution fusion | flops 1086848000 | bytes 19140608 | tf_op jit(solution)/shard_map/tgd,sd->gts/dot_general | solution.py:43
  61.9 3.7 exponential_reduce_fusion
  65.5 2.1 copy-done.2
  67.6 37.1 %all-gather.4.cloned.1.call-done = bf16[4096,128]{1,0:T(8,128)(2,1)} async-done(((bf16[256,128]{1,0:T(8,128)(2,1)}), bf16[4096,128]{1,0:T(8,128)(2,1)}) %all-gather.4.cloned.1.call-update) | async-done | bytes 1048592 | tf_op jit(solution)/shard_map/all_gather | solution.py:92
  104.7 10.0 %fusion.9 = f32[4,256]{1,0:T(4,128)S(1)} fusion(bf16[4096,128]{1,0:T(8,128)(2,1)} %all-gather.4.cloned.1.call-done, bf16[256,4,128]{0,2,1:T(8,128)(2,1)} %bitcast.86, f32[4096,256,4]{1,0,2:T(8,128)} %copy-done.2, f32[4,256]{1,0:T(4,128)S(1)} %log_add_fusion, pred[256,4096]{0,1:T(8,128)(4,1)S(1)} %bitcast_and_fusion), kind=kOutput, calls=%fused_computation.21 | convolution fusion | flops 1095105536 | bytes 19144704 | tf_op jit(solution)/shard_map/gts,sd->gtd/dot_general | solution.py:43
  114.7 0.0 copy-start.4
  114.7 9.6 %fusion.2 = bf16[4,256,4096]{1,2,0:T(8,128)(2,1)S(1)} fusion(f32[4096,256,4]{1,0,2:T(8,128)} %copy-done.2, bf16[256,4,128]{0,2,1:T(8,128)(2,1)S(1)} %bitcast.88, f32[4,256]{1,0:T(4,128)S(1)} %fusion.9, f32[4,256]{1,0:T(4,128)S(1)} %log_add_fusion, pred[256,4096]{0,1:T(8,128)(4,1)S(1)} %bitcast_and_fusion, bf16[4096,128]{1,0:T(8,128)(2,1)S(1)} %copy-done.13), kind=kOutput, calls=%fused_computation.3 | convolution fusion | flops 1107296256 | bytes 27533312 | tf_op jit(solution)/shard_map/tgd,sd->gts/dot_general | solution.py:43
  124.4 3.2 copy-done.1
  127.6 3.9 fusion.7
  131.5 0.0 reduce-scatter.5.cloned.1.call-update
  131.5 0.3 reduce-scatter.7.cloned.1.call-start
  131.8 11.4 %fusion.8 = bf16[4096,128]{1,0:T(8,128)(2,1)} fusion(bf16[256,4,128]{0,2,1:T(8,128)(2,1)} %bitcast.87, f32[4096,256,4]{1,0,2:T(8,128)} %copy-done.2, f32[4,256]{1,0:T(4,128)S(1)} %log_add_fusion, pred[256,4096]{0,1:T(8,128)(4,1)S(1)} %bitcast_and_fusion), kind=kOutput, calls=%fused_computation.17 | convolution fusion | flops 1095237632 | bytes 19140608 | tf_op jit(solution)/shard_map/gts,tgd->sd/dot_general | solution.py:43
  143.2 0.0 reduce-scatter.7.cloned.1.call-update
  143.2 0.0 reduce-scatter.11.cloned.1.call-start
  143.3 7.2 %convolution_bitcast_fusion.2 = f32[256,4,128]{2,0,1:T(8,128)S(1)} fusion(bf16[4,256,4096]{1,2,0:T(8,128)(2,1)} %copy-done.1, bf16[4096,1,128]{0,2,1:T(8,128)(2,1)} %all-gather.6.cloned.1.call-done), kind=kOutput, calls=%fused_computation.20 | convolution fusion | flops 1073741824 | bytes 9961472 | tf_op jit(solution)/shard_map/gts,sd->tgd/dot_general | solution.py:43
  150.5 0.3 subtract_convert_fusion
  150.8 0.1 pad_maximum_fusion.1
  150.9 0.1 copy.37
  151.1 46.3 %reduce-scatter.5.cloned.1.call-done = bf16[256,128]{0,1:T(8,128)(2,1)} async-done(((bf16[4096,128]{0,1:T(8,128)(2,1)}), bf16[256,128]{0,1:T(8,128)(2,1)}) %reduce-scatter.5.cloned.1.call-update) | async-done | bytes 65552 | tf_op jit(solution)/shard_map/reduce_scatter | solution.py:107
  197.3 0.8 bitcast_convert_fusion
  198.2 0.3 fusion.30
  198.5 68.9 %reduce-scatter.7.cloned.1.call-done = bf16[256,128]{1,0:T(8,128)(2,1)} async-done(((bf16[4096,128]{1,0:T(8,128)(2,1)}), bf16[256,128]{1,0:T(8,128)(2,1)}) %reduce-scatter.7.cloned.1.call-update) | async-done | bytes 65552 | tf_op jit(solution)/shard_map/reduce_scatter | solution.py:110
  267.5 0.9 copy.40
  268.4 4.5 %fusion.5 = bf16[4096,768]{0,1:T(8,128)(2,1)} fusion(bf16[256,4096]{1,0:T(8,128)(2,1)S(1)} %copy-done, bf16[256,128]{0,1:T(8,128)(2,1)S(1)} %copy.40, bf16[256,128]{0,1:T(8,128)(2,1)S(1)} %maximum_bitcast_fusion, bf16[256,512]{0,1:T(8,128)(2,1)S(1)} %bitcast.84), kind=kOutput, calls=%fused_computation.10 | convolution fusion | flops 1614938112 | bytes 8781824 | tf_op jit(solution)/shard_map/dot_general | solution.py:119
  272.9 0.0 reduce-scatter.11.cloned.1.call-update
  272.9 0.0 copy-start.3
  272.9 0.3 reduce-scatter.9.cloned.1.call-start
  273.2 2.0 fusion.50
  275.2 3.6 convolution_add_fusion
  278.9 2.1 fusion.6
  281.0 0.0 reduce-scatter.9.cloned.1.call-update
  281.0 80.8 %reduce-scatter.11.cloned.1.call-done = bf16[256,768]{0,1:T(8,128)(2,1)} async-done(((bf16[4096,768]{0,1:T(8,128)(2,1)}), bf16[256,768]{0,1:T(8,128)(2,1)}) %reduce-scatter.11.cloned.1.call-update) | async-done | bytes 393232 | tf_op jit(solution)/shard_map/reduce_scatter | solution.py:118
  361.8 1.0 slice.52
  362.8 1.0 copy.41
  363.8 0.9 fusion.54
  364.7 0.8 copy.42
  365.4 0.8 copy.43
  366.2 40.0 %reduce-scatter.9.cloned.1.call-done = bf16[256,512]{1,0:T(8,128)(2,1)} async-done(((bf16[256,4096]{1,0:T(8,128)(2,1)}), bf16[256,512]{1,0:T(8,128)(2,1)}) %reduce-scatter.9.cloned.1.call-update) | async-done | bytes 262160 | tf_op jit(solution)/shard_map/reduce_scatter | solution.py:141
  (25 shorter events, 0.1 us)
Async XLA Ops:
  7.2 1.6 copy-start
  7.2 50.2 %all-gather.6.cloned.1.call-start = ((), (), s32[]{:S(2)}) async-start(), calls=%async_computation.9 | async-start | bytes 1114112 | tf_op jit(solution)/shard_map/all_gather | solution.py:91
  7.2 9.1 %copy-start.11 = (f32[64]{0:T(128)}, f32[64]{0:T(128)S(1)}, u32[]{:S(2)}) copy-start(f32[64]{0:T(128)S(1)} %negate_power_fusion) | copy-start | bytes 772
  8.8 7.6 %copy-start.9 = (f32[256]{0:T(256)}, f32[256]{0:T(256)S(1)}, u32[]{:S(2)}) copy-start(f32[256]{0:T(256)S(1)} %convert_element_type.52) | copy-start | bytes 3076
  8.8 14.5 %copy-start.7 = (bf16[256,512]{1,0:T(8,128)(2,1)S(1)}, bf16[256,512]{1,0:T(8,128)(2,1)}, u32[]{:S(2)}) copy-start(bf16[256,512]{1,0:T(8,128)(2,1)} %param.13) | copy-start | bytes 786436
  11.9 92.9 %all-gather.4.cloned.1.call-start = ((), (), s32[]{:S(2)}) async-start(), calls=%async_computation.4 | async-start | bytes 1114112 | tf_op jit(solution)/shard_map/all_gather | solution.py:92
  14.5 182.9 %reduce-scatter.5.cloned.1.call-start = ((), (), s32[]{:S(2)}) async-start(), calls=%async_computation.5 | async-start | bytes 1114112 | tf_op jit(solution)/shard_map/reduce_scatter | solution.py:107
  61.8 5.7 %copy-start.2 = (f32[4096,256,4]{1,0,2:T(8,128)}, f32[4096,256,4]{1,0,2:T(8,128)S(1)}, u32[]{:S(2)}) copy-start(f32[4096,256,4]{1,0,2:T(8,128)S(1)} %get-tuple-element.28) | copy-start | bytes 50331652
  104.7 10.0 %copy-start.8 = (bf16[256,512]{0,1:T(8,128)(2,1)S(1)}, bf16[256,512]{0,1:T(8,128)(2,1)}, u32[]{:S(2)}) copy-start(bf16[256,512]{0,1:T(8,128)(2,1)} %copy.31) | copy-start | bytes 786436
  104.7 10.0 %copy-start.13 = (bf16[4096,128]{1,0:T(8,128)(2,1)S(1)}, bf16[4096,128]{1,0:T(8,128)(2,1)}, u32[]{:S(2)}) copy-start(bf16[4096,128]{1,0:T(8,128)(2,1)} %all-gather.4.cloned.1.call-done) | copy-start | bytes 3145732
  114.7 12.9 %copy-start.4 = (bf16[256,4,64]{2,0,1:T(8,128)(2,1)S(1)}, bf16[256,4,64]{2,0,1:T(8,128)(2,1)}, u32[]{:S(2)}) copy-start(bf16[256,4,64]{2,0,1:T(8,128)(2,1)} %get-tuple-element.13) | copy-start | bytes 393220
  124.4 3.2 copy-start.1
  131.5 135.9 %reduce-scatter.7.cloned.1.call-start = ((), (), s32[]{:S(2)}) async-start(), calls=%async_computation.6 | async-start | bytes 1114112 | tf_op jit(solution)/shard_map/reduce_scatter | solution.py:110
  143.2 7.3 %copy-start.5 = (f32[256,64]{1,0:T(8,128)S(1)}, f32[256,64]{1,0:T(8,128)}, u32[]{:S(2)}) copy-start(f32[256,64]{1,0:T(8,128)} %get-tuple-element.24) | copy-start | bytes 196612
  143.2 55.0 %copy-start.10 = (f32[256]{0:T(256)S(1)}, f32[256]{0:T(256)}, u32[]{:S(2)}) copy-start(f32[256]{0:T(256)} %copy-done.9) | copy-start | bytes 3076
  143.2 55.0 %copy-start.12 = (f32[64]{0:T(128)S(1)}, f32[64]{0:T(128)}, u32[]{:S(2)}) copy-start(f32[64]{0:T(128)} %copy-done.11) | copy-start | bytes 772
  143.2 218.6 %reduce-scatter.11.cloned.1.call-start = ((), (), s32[]{:S(2)}) async-start(), calls=%async_computation.8 | async-start | bytes 6684672 | tf_op jit(solution)/shard_map/reduce_scatter | solution.py:118
  272.9 5.9 %copy-start.3 = (bf16[4096,128]{1,0:T(8,128)(2,1)S(1)}, bf16[4096,128]{1,0:T(8,128)(2,1)}, u32[]{:S(2)}) copy-start(bf16[4096,128]{1,0:T(8,128)(2,1)} %param.10) | copy-start | bytes 3145732
  272.9 5.9 %copy-start.6 = (bf16[256,128]{1,0:T(8,128)(2,1)S(1)}, bf16[256,128]{1,0:T(8,128)(2,1)}, u32[]{:S(2)}) copy-start(bf16[256,128]{1,0:T(8,128)(2,1)} %reduce-scatter.7.cloned.1.call-done) | copy-start | bytes 196612
  272.9 133.3 %reduce-scatter.9.cloned.1.call-start = ((), (), s32[]{:S(2)}) async-start(), calls=%async_computation.7 | async-start | bytes 2359296 | tf_op jit(solution)/shard_map/reduce_scatter | solution.py:141
Sparse Core Ops, SparseCore 0:
  12.0 45.3 all-gather.5
  59.8 44.8 all-gather.3
  131.7 65.6 reduce-scatter.4
  201.4 65.9 reduce-scatter.6
  273.0 88.7 reduce-scatter.10
  364.8 41.4 reduce-scatter.8
where the time goes:
time: 414 us; the launch traced here: 413 us
  waiting for transfers between devices  302 us (73%)
  matrix products  66.8 us (16%)
  local copies, waits for them, and re-layouts  14.5 us (4%)
  other arithmetic  14.5 us (4%)
  between operations  14.4 us (3%)
    reduce_scatter x1, waiting for transfers between devices, body(): lax.psum_scatter(lax.dot_general(normed, joined, (((0,), (0,)), ((), ()))...  80.8 us
    reduce_scatter x1, waiting for transfers between devices, body(): lax.psum_scatter(grad_value.astype(jnp.bfloat16), 'seq', scatter_dimensio...  68.9 us
    dot_general x6, matrix products, product(): return jnp.einsum(form, left, right, preferred_element_type=jnp.float32)  46.6 us
    reduce_scatter x1, waiting for transfers between devices, body(): lax.psum_scatter(grad_key.astype(jnp.bfloat16), 'seq', scatter_dimension=...  46.3 us
    reduce_scatter x1, waiting for transfers between devices, body(): lax.psum_scatter(partial_input.astype(jnp.bfloat16), 'kvh', scatter_dimen...  40 us
    all_gather x1, waiting for transfers between devices, body(): lax.all_gather(values, 'seq', axis=0, tiled=True)  37.1 us
    all_gather x1, waiting for transfers between devices, body(): lax.all_gather(keys, 'seq', axis=0, tiled=True)  28.9 us
    unnamed x33, local copies, waits for them, and re-layouts  10 us
  transfers between devices with their start and end apart: 6, of which 6 were waited for; matrix products, arithmetic and copies ran while one was open for 14% of the time, Pallas kernels for 0%

commit v1 on v0

--- a/solution.py
+++ b/solution.py
@@ -1,3 +1,4 @@
+import functools
 import jax
 import jax.numpy as jnp
 from jax import lax
@@ -6,6 +7,21 @@
 HEAD = 128
 BLOCK = 128
 THETA = 500000.0
+
+
+def balance_scales_up(local_values, row_axis, k_dim):
+    return jnp.concatenate(
+        lax.all_to_all(
+            jnp.stack([local_values for _ in range(lax.axis_size(row_axis))]),
+            axis_name=row_axis,
+            split_axis=0,
+            concat_axis=0,
+        ),
+        axis=k_dim,
+    )
+
+
+views_extend = functools.partial(balance_scales_up, row_axis="seq", k_dim=0)
 
 
 def rotate(values, positions, rotation_sign):
@@ -87,10 +103,7 @@
         jnp.dot(normed, w_key, preferred_element_type=jnp.float32), positions, 1.0
     ).astype(jnp.bfloat16)
     values = jnp.dot(normed, w_value, preferred_element_type=jnp.float32).astype(jnp.bfloat16)
-    keys_all, values_all = (
-        lax.all_gather(keys, "seq", axis=0, tiled=True),
-        lax.all_gather(values, "seq", axis=0, tiled=True),
-    )
+    keys_all, values_all = (lax.all_gather(keys, "seq", axis=0, tiled=True), views_extend(values))
     seen = visible(block_mask, my_index * blk_local, tok_rows, keys_all.shape[0])
     total_parts = []
     dots_parts = []

time: 414 us -> 383 us (0.925)
  waiting for transfers between devices: 302 us -> 267 us
  starting transfers between devices: 0.73 us -> 8.47 us
    all_gather x1 -> x0, waiting for transfers between devices: 37.1 us -> none  [body(): lax.all_gather(values, 'seq', axis=0, tiled=True)]
    all_to_all x0 -> x1, starting transfers between devices: none -> 8.01 us  [balance_scales_up(): lax.all_to_all(jnp.stack([local_values for _ in range(lax.axis_size(row_a...]
    unnamed x33 -> x27, local copies, waits for them, and re-layouts: 10 us -> 9.41 us
  transfers between devices with their start and end apart: 6 -> 6, of which waited for: 6 -> 5; matrix products, arithmetic and copies ran while one was open for 14% -> 14% of each run, Pallas kernels for 0% -> 0%
where the time goes in v1:
time: 383 us; the launch traced here: 382 us
  waiting for transfers between devices  267 us (70%)
  matrix products  67.1 us (18%)
  local copies, waits for them, and re-layouts  14.3 us (4%)
  between operations  14.1 us (4%)
  other arithmetic  11.8 us (3%)
  starting transfers between devices  8.47 us (2%)
    reduce_scatter x1, waiting for transfers between devices, body(): lax.psum_scatter(lax.dot_general(normed, joined, (((0,), (0,)), ((), ()))...  81.1 us
    reduce_scatter x1, waiting for transfers between devices, body(): lax.psum_scatter(grad_value.astype(jnp.bfloat16), 'seq', scatter_dimensio...  69.1 us
    reduce_scatter x1, waiting for transfers between devices, body(): lax.psum_scatter(grad_key.astype(jnp.bfloat16), 'seq', scatter_dimension=...  47.5 us
    dot_general x6, matrix products, product(): return jnp.einsum(form, left, right, preferred_element_type=jnp.float32)  47.5 us
    reduce_scatter x1, waiting for transfers between devices, body(): lax.psum_scatter(partial_input.astype(jnp.bfloat16), 'kvh', scatter_dimen...  40.1 us
    all_gather x1, waiting for transfers between devices, body(): lax.all_gather(keys, 'seq', axis=0, tiled=True)  28.9 us
    unnamed x27, local copies, waits for them, and re-layouts  9.41 us
    all_to_all x1, starting transfers between devices, balance_scales_up(): lax.all_to_all(jnp.stack([local_values for _ in range(lax.axis_size(row_a...  8.01 us
  transfers between devices with their start and end apart: 6, of which 5 were waited for; matrix products, arithmetic and copies ran while one was open for 14% of the time, Pallas kernels for 0%

profile of v1, /device:TPU:0, one launch (start us, length us, event | category | flops | bytes accessed | tf_op | source)
XLA Modules:
  0.0 382.4 jit_solution(11888233251317039786)
XLA Ops:
  7.2 0.0 copy-start
  7.2 0.0 all-gather.3.cloned.1.call-start
  7.2 0.8 convert_element_type.52
  8.1 0.7 copy-done
  8.8 2.0 convolution_bitcast_fusion.3
  10.8 0.0 copy-start.10
  10.8 0.0 copy-start.8
  10.9 0.3 fusion.32
  11.2 0.6 pad_maximum_fusion.2
  11.8 0.0 all-gather.3.cloned.1.call-update
  11.8 1.9 convolution_convert_fusion.1
  13.8 1.2 stack.2
  15.0 8.0 %all-to-all-start = ((bf16[16,256,128]{2,1,0:T(8,128)(2,1)}), bf16[16,256,128]{2,1,0:T(8,128)(2,1)}, u32[]{:S(2)}, u32[]{:S(2)}) async-start(bf16[16,256,128]{2,1,0:T(8,128)(2,1)} %stack.2), calls=%async_computation | async-start | bytes 2097152 | tf_op jit(solution)/shard_map/all_to_all | solution.py:14
  23.0 0.0 reduce-scatter.5.cloned.1.call-start
  23.0 3.5 fusion.53
  26.5 0.2 reshape.298
  26.7 0.1 copy.27
  26.8 0.1 broadcast_in_dim.30
  27.0 0.8 copy.31
  27.8 2.7 bitcast_and_fusion
  30.5 1.2 broadcast_multiply_fusion
  31.7 0.3 fusion.51
  32.0 0.8 subtract_convert_fusion.1
  32.9 28.9 %all-gather.3.cloned.1.call-done = bf16[4096,1,128]{0,2,1:T(8,128)(2,1)} async-done(((bf16[256,1,128]{0,2,1:T(8,128)(2,1)}), bf16[4096,1,128]{0,2,1:T(8,128)(2,1)}) %all-gather.3.cloned.1.call-update) | async-done | bytes 1048592 | tf_op jit(solution)/shard_map/all_gather | solution.py:106
  61.7 4.9 %fusion.4 = (f32[4,256]{1,0:T(4,128)S(1)}, f32[4096,256,4]{1,0,2:T(8,128)S(1)}) fusion(pred[256,4096]{0,1:T(8,128)(4,1)} %bitcast_and_fusion, bf16[256,4,64]{2,0,1:T(8,128)(2,1)} %get-tuple-element.13, bf16[256,4,64]{2,0,1:T(8,128)(2,1)S(1)} %get-tuple-element.12, bf16[4096,1,128]{0,2,1:T(8,128)(2,1)} %all-gather.3.cloned.1.call-done), kind=kOutput, calls=%fused_computation.8 | convolution fusion | flops 1086848000 | bytes 19140608 | tf_op jit(solution)/shard_map/tgd,sd->gts/dot_general | solution.py:59
  66.7 3.7 exponential_reduce_fusion
  70.3 2.1 copy-done.2
  72.4 0.0 all-to-all-done
  72.4 0.0 copy-start.9
  72.4 10.0 %fusion.9 = f32[4,256]{1,0:T(4,128)S(1)} fusion(bf16[4096,128,1]{1,0,2:T(8,128)(2,1)} %bitcast.7, bf16[256,4,128]{0,2,1:T(8,128)(2,1)} %bitcast.86, f32[4096,256,4]{1,0,2:T(8,128)} %copy-done.2, f32[4,256]{1,0:T(4,128)S(1)} %log_add_fusion, pred[256,4096]{0,1:T(8,128)(4,1)S(1)} %copy-done.4), kind=kOutput, calls=%fused_computation.21 | convolution fusion | flops 1095105536 | bytes 19144704 | tf_op jit(solution)/shard_map/gts,sd->gtd/dot_general | solution.py:59
  82.4 0.0 copy-start.5
  82.4 10.1 %fusion.2 = bf16[4,256,4096]{1,2,0:T(8,128)(2,1)S(1)} fusion(f32[4096,256,4]{1,0,2:T(8,128)} %copy-done.2, bf16[4096,128,1]{1,0,2:T(8,128)(2,1)} %bitcast.7, bf16[256,4,128]{0,2,1:T(8,128)(2,1)S(1)} %bitcast.88, f32[4,256]{1,0:T(4,128)S(1)} %fusion.9, f32[4,256]{1,0:T(4,128)S(1)} %log_add_fusion, pred[256,4096]{0,1:T(8,128)(4,1)S(1)} %copy-done.4), kind=kOutput, calls=%fused_computation.3 | convolution fusion | flops 1107296256 | bytes 27533312 | tf_op jit(solution)/shard_map/tgd,sd->gts/dot_general | solution.py:59
  92.5 3.2 copy-done.1
  95.7 3.9 %fusion.7 = bf16[4096,128]{0,1:T(8,128)(2,1)} fusion(bf16[4,256,4096]{1,2,0:T(8,128)(2,1)S(1)} %fusion.2, bf16[256,4,64]{2,0,1:T(8,128)(2,1)S(1)} %copy-done.5, bf16[256,4,64]{2,0,1:T(8,128)(2,1)S(1)} %get-tuple-element.12), kind=kOutput, calls=%fused_computation.16 | convolution fusion | flops 1074790400 | bytes 9699328 | tf_op jit(solution)/shard_map/gts,tgd->sd/dot_general | solution.py:59
  99.6 0.0 reduce-scatter.5.cloned.1.call-update
  99.6 0.0 reduce-scatter.7.cloned.1.call-start
  99.7 11.4 %fusion.8 = bf16[4096,128]{1,0:T(8,128)(2,1)} fusion(bf16[256,4,128]{0,2,1:T(8,128)(2,1)} %bitcast.87, f32[4096,256,4]{1,0,2:T(8,128)} %copy-done.2, f32[4,256]{1,0:T(4,128)S(1)} %log_add_fusion, pred[256,4096]{0,1:T(8,128)(4,1)S(1)} %copy-done.4), kind=kOutput, calls=%fused_computation.17 | convolution fusion | flops 1095237632 | bytes 19140608 | tf_op jit(solution)/shard_map/gts,tgd->sd/dot_general | solution.py:59
  111.1 0.0 reduce-scatter.7.cloned.1.call-update
  111.1 0.3 reduce-scatter.11.cloned.1.call-start
  111.4 7.2 %convolution_bitcast_fusion.2 = f32[256,4,128]{2,0,1:T(8,128)S(1)} fusion(bf16[4,256,4096]{1,2,0:T(8,128)(2,1)} %copy-done.1, bf16[4096,1,128]{0,2,1:T(8,128)(2,1)} %all-gather.3.cloned.1.call-done), kind=kOutput, calls=%fused_computation.20 | convolution fusion | flops 1073741824 | bytes 9961472 | tf_op jit(solution)/shard_map/gts,sd->tgd/dot_general | solution.py:59
  118.7 0.3 subtract_convert_fusion
  118.9 0.1 pad_maximum_fusion.1
  119.1 0.1 copy.37
  119.2 47.5 %reduce-scatter.5.cloned.1.call-done = bf16[256,128]{0,1:T(8,128)(2,1)} async-done(((bf16[4096,128]{0,1:T(8,128)(2,1)}), bf16[256,128]{0,1:T(8,128)(2,1)}) %reduce-scatter.5.cloned.1.call-update) | async-done | bytes 65552 | tf_op jit(solution)/shard_map/reduce_scatter | solution.py:120
  166.7 0.8 bitcast_convert_fusion
  167.6 0.3 fusion.28
  167.9 69.1 %reduce-scatter.7.cloned.1.call-done = bf16[256,128]{1,0:T(8,128)(2,1)} async-done(((bf16[4096,128]{1,0:T(8,128)(2,1)}), bf16[256,128]{1,0:T(8,128)(2,1)}) %reduce-scatter.7.cloned.1.call-update) | async-done | bytes 65552 | tf_op jit(solution)/shard_map/reduce_scatter | solution.py:123
  237.0 0.9 copy.40
  238.0 4.5 %fusion.5 = bf16[4096,768]{0,1:T(8,128)(2,1)} fusion(bf16[256,4096]{1,0:T(8,128)(2,1)S(1)} %copy-done, bf16[256,128]{0,1:T(8,128)(2,1)S(1)} %copy.40, bf16[256,128]{0,1:T(8,128)(2,1)S(1)} %maximum_bitcast_fusion, bf16[256,512]{0,1:T(8,128)(2,1)S(1)} %bitcast.84), kind=kOutput, calls=%fused_computation.10 | convolution fusion | flops 1614938112 | bytes 8781824 | tf_op jit(solution)/shard_map/dot_general | solution.py:132
  242.4 0.0 reduce-scatter.11.cloned.1.call-update
  242.5 0.0 copy-start.3
  242.5 0.0 copy-start.7
  242.5 0.0 reduce-scatter.9.cloned.1.call-start
  242.5 2.0 fusion.48
  244.6 3.6 convolution_add_fusion
  248.2 2.1 fusion.6
  250.3 0.0 reduce-scatter.9.cloned.1.call-update
  250.3 81.1 %reduce-scatter.11.cloned.1.call-done = bf16[256,768]{0,1:T(8,128)(2,1)} async-done(((bf16[4096,768]{0,1:T(8,128)(2,1)}), bf16[256,768]{0,1:T(8,128)(2,1)}) %reduce-scatter.11.cloned.1.call-update) | async-done | bytes 393232 | tf_op jit(solution)/shard_map/reduce_scatter | solution.py:131
  331.4 1.0 slice.52
  332.4 1.0 copy.41
  333.4 0.9 fusion.52
  334.3 0.8 copy.42
  335.0 0.8 copy.43
  335.8 40.1 %reduce-scatter.9.cloned.1.call-done = bf16[256,512]{1,0:T(8,128)(2,1)} async-done(((bf16[256,4096]{1,0:T(8,128)(2,1)}), bf16[256,512]{1,0:T(8,128)(2,1)}) %reduce-scatter.9.cloned.1.call-update) | async-done | bytes 262160 | tf_op jit(solution)/shard_map/reduce_scatter | solution.py:154
  (19 shorter events, 0.1 us)
Async XLA Ops:
  7.2 1.6 copy-start
  7.2 54.5 %all-gather.3.cloned.1.call-start = ((), (), s32[]{:S(2)}) async-start(), calls=%async_computation.9 | async-start | bytes 1114112 | tf_op jit(solution)/shard_map/all_gather | solution.py:106
  10.8 15.9 %copy-start.10 = (s32[2,32]{1,0:T(2,128)S(1)}, s32[2,32]{1,0:T(2,128)}, u32[]{:S(2)}) copy-start(s32[2,32]{1,0:T(2,128)} %param.12) | copy-start | bytes 772
  10.8 16.1 %copy-start.8 = (bf16[256,512]{1,0:T(8,128)(2,1)S(1)}, bf16[256,512]{1,0:T(8,128)(2,1)}, u32[]{:S(2)}) copy-start(bf16[256,512]{1,0:T(8,128)(2,1)} %param.13) | copy-start | bytes 786436
  15.0 57.4 %all-to-all-start = ((bf16[16,256,128]{2,1,0:T(8,128)(2,1)}), bf16[16,256,128]{2,1,0:T(8,128)(2,1)}, u32[]{:S(2)}, u32[]{:S(2)}) async-start(bf16[16,256,128]{2,1,0:T(8,128)(2,1)} %stack.2), calls=%async_computation | async-start | bytes 2097152 | tf_op jit(solution)/shard_map/all_to_all | solution.py:14
  23.0 143.7 %reduce-scatter.5.cloned.1.call-start = ((), (), s32[]{:S(2)}) async-start(), calls=%async_computation.5 | async-start | bytes 1114112 | tf_op jit(solution)/shard_map/reduce_scatter | solution.py:120
  61.7 4.9 %copy-start.4 = (pred[256,4096]{0,1:T(8,128)(4,1)S(1)}, pred[256,4096]{0,1:T(8,128)(4,1)}, u32[]{:S(2)}) copy-start(pred[256,4096]{0,1:T(8,128)(4,1)} %bitcast_and_fusion) | copy-start | bytes 3145732
  66.6 5.7 %copy-start.2 = (f32[4096,256,4]{1,0,2:T(8,128)}, f32[4096,256,4]{1,0,2:T(8,128)S(1)}, u32[]{:S(2)}) copy-start(f32[4096,256,4]{1,0,2:T(8,128)S(1)} %get-tuple-element.28) | copy-start | bytes 50331652
  72.4 10.0 %copy-start.9 = (bf16[256,512]{0,1:T(8,128)(2,1)S(1)}, bf16[256,512]{0,1:T(8,128)(2,1)}, u32[]{:S(2)}) copy-start(bf16[256,512]{0,1:T(8,128)(2,1)} %copy.31) | copy-start | bytes 786436
  82.4 13.3 %copy-start.5 = (bf16[256,4,64]{2,0,1:T(8,128)(2,1)S(1)}, bf16[256,4,64]{2,0,1:T(8,128)(2,1)}, u32[]{:S(2)}) copy-start(bf16[256,4,64]{2,0,1:T(8,128)(2,1)} %get-tuple-element.13) | copy-start | bytes 393220
  92.5 3.2 copy-start.1
  99.6 137.4 %reduce-scatter.7.cloned.1.call-start = ((), (), s32[]{:S(2)}) async-start(), calls=%async_computation.6 | async-start | bytes 1114112 | tf_op jit(solution)/shard_map/reduce_scatter | solution.py:123
  111.1 7.6 %copy-start.6 = (f32[256,64]{1,0:T(8,128)S(1)}, f32[256,64]{1,0:T(8,128)}, u32[]{:S(2)}) copy-start(f32[256,64]{1,0:T(8,128)} %get-tuple-element.24) | copy-start | bytes 196612
  111.1 220.3 %reduce-scatter.11.cloned.1.call-start = ((), (), s32[]{:S(2)}) async-start(), calls=%async_computation.8 | async-start | bytes 6684672 | tf_op jit(solution)/shard_map/reduce_scatter | solution.py:131
  242.5 5.7 %copy-start.3 = (bf16[4096,128]{1,0:T(8,128)(2,1)S(1)}, bf16[4096,128]{1,0:T(8,128)(2,1)}, u32[]{:S(2)}) copy-start(bf16[4096,128]{1,0:T(8,128)(2,1)} %param.10) | copy-start | bytes 3145732
  242.5 5.7 %copy-start.7 = (bf16[256,128]{1,0:T(8,128)(2,1)S(1)}, bf16[256,128]{1,0:T(8,128)(2,1)}, u32[]{:S(2)}) copy-start(bf16[256,128]{1,0:T(8,128)(2,1)} %reduce-scatter.7.cloned.1.call-done) | copy-start | bytes 196612
  242.5 133.4 %reduce-scatter.9.cloned.1.call-start = ((), (), s32[]{:S(2)}) async-start(), calls=%async_computation.7 | async-start | bytes 2359296 | tf_op jit(solution)/shard_map/reduce_scatter | solution.py:154
Sparse Core Ops, SparseCore 0:
  12.0 49.7 all-gather.2
  99.8 66.9 reduce-scatter.4
  171.0 65.9 reduce-scatter.6
  242.6 88.7 reduce-scatter.10
  334.3 41.4 reduce-scatter.8
